TPU v7x, 512 devices: a whole 4x8x8 slice. The times are simulated.
512 devices in a mesh: req: 64 (over z, x, core), tp: 8 (over y).
Axes of the slice: x: 4, y: 8, z: 8, core: 2. Of those that a mesh axis runs over, the one named last changes fastest.
Arguments:
- queries: bfloat16 [1024, 2048], P('req', 'tp'), may hold values from -27 to 27
- fresh_cache: bfloat16 [1024, 2, 2048], P('req', None, 'tp'), may hold values from -4 to 4
- tail_cache: bfloat16 [1024, 32, 2, 2048], P('req', None, None, 'tp'), may hold values from -4 to 4
- tail_len: int32 [1024], P('req'), may hold values from 1 to 32, as said below
- pool_cache: bfloat16 [2048, 64, 2, 2048], P('req', None, None, 'tp'), may hold values from -4 to 4
- page_group: int32 [2048], P('req'), may hold values from 0 to 63, as said below
- page_start: int32 [2048], P('req'), may hold values from 0 to 16320, as said below
- prompt_len: int32 [64], replicated, may hold values from 1 to 16384, as said below
- residual: bfloat16 [1024, 2048], P('req'), may hold values from -80 to 80
- out_weight: bfloat16 [2048, 2048], P('tp'), may hold values from -0.125 to 0.125
- out_bias: bfloat16 [2048], replicated, may hold values from -0.796875 to 0.796875
- norm_gain: bfloat16 [2048], P('tp'), may hold values from 0.5 to 1.5
- norm_shift: bfloat16 [2048], P('tp'), may hold values from -0.796875 to 0.796875
Outputs:
- attention_out: bfloat16 [1024, 2048], P('req', 'tp')
- normed: bfloat16 [1024, 2048], P('req', 'tp')
Inputs may be any that keep to these rules, and one draw needn't show every extreme that they name: page_group[p] is the group whose prompt page p holds; every page holds some group's prompt; every group holds at least one page and at most 256 pages, and some group holds exactly 256; the pages of a group of n pages lie on min(n, 64) different indices of req, none holding more than ceil(n / 64) of them. The pages of a group of n pages have page_start 0, 64, ..., (n - 1) * 64, each once. `prompt_len`: a group of n pages has a prompt of (n - 1) * 64 + 1 to n * 64 positions. `tail_len`: some request has exactly 32 tail positions.
All inputs are finite; a program needn't handle non-finite values.
Results may differ from a plain program's by a relative error of at most 0.02.
Values may be sent and summed in bfloat16 or wider, within the bound.
No kernel may reach another device: no remote copies, remote signals or barrier semaphores. Data moves between devices by JAX's collectives and lax.ppermute only.
A program may use at most 64 MiB of HBM per device.

v0:
```python
import math
import jax
import jax.numpy as jnp
from jax import lax
from jax.sharding import PartitionSpec as P

HEADS = 16
HEAD = 128
PAGE = 64
masked_score = -1e30
norm_epsilon = 1e-05


def split_halves(values):
    upper_part = lax.optimization_barrier(values.astype(jnp.bfloat16))
    lower_part = (values - upper_part.astype(jnp.float32)).astype(jnp.bfloat16)
    return (upper_part, lower_part)


def local(
    queries,
    fresh_cache,
    tail_cache,
    tail_len,
    pool_cache,
    page_group,
    page_start,
    prompt_len,
    residual,
    out_weight,
    out_bias,
    norm_gain,
    norm_shift,
):
    f32 = jnp.float32
    highest = lax.Precision.HIGHEST
    row_count, feat_width = queries.shape
    heads_here = feat_width // HEAD
    inv_root = 1.0 / math.sqrt(HEAD)
    head_ids = lax.axis_index("tp") * heads_here + jnp.arange(heads_here)
    slopes = jnp.exp2(-8.0 * (head_ids.astype(f32) + 1.0) / HEADS)
    group_count = prompt_len.shape[0]
    page_count = pool_cache.shape[0]
    tail_slots = tail_cache.shape[1]
    n_req = lax.axis_size("req")
    assert group_count == n_req
    everyone = lax.all_gather(queries, "req", axis=0, tiled=True)
    by_group = everyone.reshape(group_count, row_count, heads_here, HEAD)
    safe_group = jnp.clip(page_group, 0, group_count - 1)
    page_queries = by_group[safe_group]
    page_keys = pool_cache[:, :, 0].reshape(page_count, PAGE, heads_here, HEAD)
    page_values = pool_cache[:, :, 1].reshape(page_count, PAGE, heads_here, HEAD)
    prompt_here = prompt_len[safe_group]
    positions = page_start[:, None] + jnp.arange(PAGE)[None, :]
    usable = (positions < prompt_here[:, None]) & (page_group[:, None] >= 0)
    offsets = (positions - prompt_here[:, None]).astype(f32)
    scores = (
        jnp.einsum("pqhd,pshd->pqhs", page_queries, page_keys, preferred_element_type=f32)
        * inv_root
    )
    scores = scores + slopes[None, None, :, None] * offsets[:, None, None, :]
    scores = jnp.where(usable[:, None, None, :], scores, masked_score)
    member = (page_group[:, None] == jnp.arange(group_count)[None, :]) & (page_group[:, None] >= 0)
    page_top = scores.max(-1)
    local_top = jnp.where(member[:, :, None, None], page_top[:, None], masked_score).max(0)
    page_ref = local_top[safe_group]
    weights = jnp.where(usable[:, None, None, :], jnp.exp(scores - page_ref[..., None]), 0.0)
    page_totals = weights.sum(-1)
    upper_part, lower_part = split_halves(weights)
    page_accum = jnp.einsum("pqhs,pshd->pqhd", upper_part, page_values, preferred_element_type=f32)
    page_accum = page_accum + jnp.einsum(
        "pqhs,pshd->pqhd", lower_part, page_values, preferred_element_type=f32
    )
    accum_upper, accum_lower = split_halves(page_accum.reshape(page_count, -1))
    spread = member.T.astype(jnp.bfloat16)
    group_accum = jnp.dot(spread, accum_upper, preferred_element_type=f32)
    group_accum = group_accum + jnp.dot(spread, accum_lower, preferred_element_type=f32)
    group_totals = jnp.dot(
        member.T.astype(f32), page_totals.reshape(page_count, -1), precision=highest
    )
    stats_width = row_count * heads_here
    pad_width = -(group_accum.shape[1] + 2 * stats_width) % 128
    packed = jnp.concatenate(
        [
            group_accum,
            local_top.reshape(group_count, stats_width),
            group_totals,
            jnp.zeros((group_count, pad_width), f32),
        ],
        axis=1,
    )
    arrived = lax.all_to_all(packed, "req", 0, 0, tiled=True)
    accum_width = row_count * feat_width
    part_accum = arrived[:, :accum_width].reshape(n_req, row_count, heads_here, HEAD)
    part_top = arrived[:, accum_width : accum_width + stats_width].reshape(
        n_req, row_count, heads_here
    )
    part_totals = arrived[:, accum_width + stats_width : accum_width + 2 * stats_width].reshape(
        n_req, row_count, heads_here
    )
    home_queries = queries.reshape(row_count, heads_here, HEAD)
    tail_keys = tail_cache[:, :, 0].reshape(row_count, tail_slots, heads_here, HEAD)
    tail_values = tail_cache[:, :, 1].reshape(row_count, tail_slots, heads_here, HEAD)
    fresh_keys = fresh_cache[:, 0].reshape(row_count, heads_here, HEAD)
    fresh_values = fresh_cache[:, 1].reshape(row_count, heads_here, HEAD)
    slot_ids = jnp.arange(tail_slots)
    tail_scores = (
        jnp.einsum("qhd,qjhd->qhj", home_queries, tail_keys, preferred_element_type=f32) * inv_root
    )
    tail_scores = tail_scores + slopes[None, :, None] * slot_ids.astype(f32)[None, None, :]
    tail_scores = jnp.where(
        slot_ids[None, None, :] < tail_len[:, None, None], tail_scores, masked_score
    )
    own_scores = (
        jnp.einsum("qhd,qhd->qh", home_queries, fresh_keys, preferred_element_type=f32) * inv_root
    )
    own_scores = own_scores + slopes[None, :] * tail_len.astype(f32)[:, None]
    home_top = jnp.maximum(tail_scores.max(-1), own_scores)
    row_top = jnp.maximum(home_top, part_top.max(0))
    part_scale = jnp.exp(part_top - row_top[None])
    pool_totals = jnp.sum(part_scale * part_totals, 0)
    pool_accum = jnp.sum(part_scale[..., None] * part_accum, 0)
    tail_weights = jnp.exp(tail_scores - row_top[:, :, None])
    own_weights = jnp.exp(own_scores - row_top)
    totals = tail_weights.sum(-1) + own_weights
    upper_part, lower_part = split_halves(tail_weights)
    accum = jnp.einsum("qhj,qjhd->qhd", upper_part, tail_values, preferred_element_type=f32)
    accum = accum + jnp.einsum("qhj,qjhd->qhd", lower_part, tail_values, preferred_element_type=f32)
    home_accum = accum + own_weights[:, :, None] * fresh_values.astype(f32)
    attention = ((pool_accum + home_accum) / (pool_totals + totals)[:, :, None]).astype(
        jnp.bfloat16
    )
    attention = attention.reshape(row_count, feat_width)
    partial_value = jnp.dot(attention, out_weight, preferred_element_type=f32)
    model_width = residual.shape[1]
    own_start = lax.axis_index("tp") * feat_width
    summed = lax.psum_scatter(
        partial_value.astype(jnp.bfloat16), "tp", scatter_dimension=1, tiled=True
    ).astype(jnp.float32)
    bias_mine = lax.dynamic_slice_in_dim(out_bias, own_start, feat_width, 0).astype(f32)
    attention_mine = (summed + bias_mine[None, :]).astype(jnp.bfloat16)
    residual_mine = lax.dynamic_slice_in_dim(residual, own_start, feat_width, 1).astype(f32)
    hidden_mine = residual_mine + attention_mine.astype(f32)
    first_sum, second_sum = lax.psum(
        (jnp.sum(hidden_mine, -1), jnp.sum(hidden_mine * hidden_mine, -1)), "tp"
    )
    row_mean = (first_sum / model_width)[:, None]
    mean_square = (second_sum / model_width)[:, None]
    row_var = mean_square - row_mean * row_mean
    normed = (
        (hidden_mine - row_mean)
        * lax.rsqrt(row_var + norm_epsilon)
        * norm_gain.astype(f32)[None, :]
    )
    normed = normed + norm_shift.astype(f32)[None, :]
    return (attention_mine, normed.astype(jnp.bfloat16))


def solution(mesh):
    in_specs = (
        P("req", "tp"),
        P("req", None, "tp"),
        P("req", None, None, "tp"),
        P("req"),
        P("req", None, None, "tp"),
        P("req"),
        P("req"),
        P(),
        P("req", None),
        P("tp", None),
        P(),
        P("tp"),
        P("tp"),
    )
    out_specs = (P("req", "tp"), P("req", "tp"))
    return jax.shard_map(local, mesh=mesh, in_specs=in_specs, out_specs=out_specs, check_vma=False)
```

profile of v0, /device:TPU:2, one launch (start us, length us, event | category | flops | bytes accessed | tf_op | source)
XLA Modules:
  0.0 193.3 jit_solution(1942544731091071462)
XLA Ops:
  7.2 0.7 compare_select_fusion
  7.9 0.7 broadcast_compare_fusion
  8.6 1.4 gather_fusion
  10.0 0.7 subtract_convert_fusion.5
  10.7 0.8 fusion.33
  11.5 56.0 %all_gather.3 = bf16[1024,256]{1,0:T(8,128)(2,1)S(1)} all-gather(bf16[16,256]{1,0:T(8,128)(2,1)} %param.13), channel_id=1, replica_groups=mesh['req'=64,'tp'=8] {'req'}, dimensions={0}, use_global_device_ids=true | all-gather | bytes 532480 | tf_op jit(solution)/shard_map/all_gather | solution.py:47
  67.5 0.1 reshape.244
  67.7 0.1 copy.47
  67.7 0.6 gather_fusion.1
  68.3 10.7 %slice_reduce_fusion = (bf16[32,64,256]{2,1,0:T(8,128)(2,1)S(1)}, bf16[32,64,256]{2,1,0:T(8,128)(2,1)S(1)}) fusion(bf16[32,64,2,256]{3,2,1,0:T(2,128)(2,1)} %param.17), kind=kLoop, calls=%fused_computation.7 | loop fusion | bytes 4194304 | tf_op jit(solution)/shard_map/slice | solution.py:52
  79.0 0.1 broadcast_multiply_fusion
  79.1 0.8 fusion.50
  79.9 0.2 select_reduce_fusion
  80.1 0.1 copy.49
  80.2 0.6 gather_fusion.2
  80.8 0.4 fusion.12
  81.2 0.4 fusion.6
  81.6 0.5 fusion.1
  82.1 0.3 copy.52
  82.4 0.4 reshape.245
  82.9 0.4 fusion.48
  83.3 0.4 convolution_add_fusion
  83.7 0.1 copy.54
  83.8 0.3 fusion.42
  84.1 0.1 copy.55
  84.2 0.3 concatenate.3
  84.5 2.1 %copy.57 = f32[64,1,4224]{2,1,0:T(1,128)} copy(f32[64,1,4224]{2,0,1:T(8,128)S(1)} %bitcast.87) | data formatting | bytes 2162688 | tf_op jit(solution)/shard_map/all_to_all | solution.py:92
  86.6 6.3 %all-to-all-start = ((f32[64,1,4224]{2,1,0:T(1,128)}), f32[64,1,4224]{2,1,0:T(1,128)}, u32[]{:S(2)}, u32[]{:S(2)}) async-start(f32[64,1,4224]{2,1,0:T(1,128)} %copy.57), calls=%async_computation | async-start | bytes 2162688 | tf_op jit(solution)/shard_map/all_to_all | solution.py:92
  93.0 0.2 reduce-scatter.2.cloned.1.call-start
  93.3 0.1 fusion.27
  93.4 0.1 copy.72
  93.6 0.1 iota_compare_fusion.1
  93.7 2.2 %slice_reduce_fusion.2 = (bf16[16,32,256]{2,1,0:T(8,128)(2,1)S(1)}, bf16[16,32,256]{2,1,0:T(8,128)(2,1)S(1)}) fusion(bf16[16,32,2,256]{3,2,1,0:T(2,128)(2,1)S(1)} %copy-done.1), kind=kLoop, calls=%fused_computation.22 | loop fusion | bytes 1048576 | tf_op jit(solution)/shard_map/slice | solution.py:103
  95.8 0.2 fusion.18
  96.1 0.1 fusion.44
  96.2 26.2 %all-to-all-done = f32[64,1,4224]{2,1,0:T(1,128)} async-done(((f32[64,1,4224]{2,1,0:T(1,128)}), f32[64,1,4224]{2,1,0:T(1,128)}, u32[]{:S(2)}, u32[]{:S(2)}) %all-to-all-start) | async-done | bytes 1081376 | tf_op jit(solution)/shard_map/all_to_all | solution.py:92
  122.4 3.1 %copy.58 = f32[64,1,4224]{0,2,1:T(8,128)S(1)} copy(f32[64,1,4224]{2,1,0:T(1,128)} %all-to-all-done) | data formatting | bytes 2162688 | tf_op jit(solution)/shard_map/all_to_all | solution.py:92
  125.5 0.1 slice_reduce_fusion.5
  125.6 0.1 reduce_max.42
  125.7 0.1 copy.59
  125.8 0.1 maximum_maximum_fusion
  125.9 0.1 fusion.38
  126.0 0.1 copy.60
  126.0 0.2 fusion.37
  126.2 0.1 sub.80
  126.3 0.7 fusion.26
  127.0 0.7 reduce_sum.62
  127.7 0.6 copy.63
  128.4 1.3 add_add_fusion
  129.7 0.8 copy.61
  130.5 0.8 copy.64
  131.2 0.2 fusion.14
  131.4 0.2 fusion.16
  131.6 0.1 subtract_exponential_fusion.1
  131.7 0.6 fusion
  132.3 0.1 fusion.35
  132.4 0.9 convolution_convert_fusion
  133.3 0.7 convert_element_type.119
  134.0 0.7 convert_element_type.120
  134.7 0.8 dynamic-slice_convert_fusion
  135.4 33.2 %reduce-scatter.2.cloned.1.call-done = bf16[16,256]{1,0:T(8,128)(2,1)} async-done(((bf16[16,2048]{1,0:T(8,128)(2,1)}), bf16[16,256]{1,0:T(8,128)(2,1)}) %reduce-scatter.2.cloned.1.call-update) | async-done | bytes 8208 | tf_op jit(solution)/shard_map/reduce_scatter | solution.py:137
  168.6 0.8 fusion.36
  169.4 15.6 %all-reduce = (f32[16]{0:T(128)S(1)}, f32[16]{0:T(128)S(1)}) all-reduce(f32[16]{0:T(128)S(1)} %get-tuple-element.7, f32[16]{0:T(128)S(1)} %get-tuple-element.6), channel_id=1, replica_groups=mesh['req'=64,'tp'=8] {'tp'}, use_global_device_ids=true, to_apply=%region_12.13 | all-reduce | flops 32 | bytes 256 | tf_op jit(solution)/shard_map/psum | solution.py:144
  185.0 1.4 add_convert_fusion
  (30 shorter events, 0.3 us)
Async XLA Ops:
  7.2 125.3 %copy-start = (bf16[256,2048]{1,0:T(8,128)(2,1)S(1)}, bf16[256,2048]{1,0:T(8,128)(2,1)}, u32[]{:S(2)}) copy-start(bf16[256,2048]{1,0:T(8,128)(2,1)} %param.22) | copy-start | bytes 3145732
  82.1 0.8 copy-start.5
  84.4 8.8 %copy-start.2 = (bf16[16,256]{1,0:T(8,128)(2,1)S(1)}, bf16[16,256]{1,0:T(8,128)(2,1)}, u32[]{:S(2)}) copy-start(bf16[16,256]{1,0:T(8,128)(2,1)} %param.13) | copy-start | bytes 24580
  84.4 8.8 %copy-start.3 = (bf16[16,2,256]{2,1,0:T(2,128)(2,1)S(1)}, bf16[16,2,256]{2,1,0:T(2,128)(2,1)}, u32[]{:S(2)}) copy-start(bf16[16,2,256]{2,1,0:T(2,128)(2,1)} %param.14) | copy-start | bytes 49156
  84.4 9.1 %copy-start.7 = (s32[16]{0:T(128)S(1)}, s32[16]{0:T(128)}, u32[]{:S(2)}) copy-start(s32[16]{0:T(128)} %param.16) | copy-start | bytes 196
  84.5 9.2 %copy-start.1 = (bf16[16,32,2,256]{3,2,1,0:T(2,128)(2,1)S(1)}, bf16[16,32,2,256]{3,2,1,0:T(2,128)(2,1)}, u32[]{:S(2)}) copy-start(bf16[16,32,2,256]{3,2,1,0:T(2,128)(2,1)} %param.15) | copy-start | bytes 1572868
  86.6 35.8 %all-to-all-start = ((f32[64,1,4224]{2,1,0:T(1,128)}), f32[64,1,4224]{2,1,0:T(1,128)}, u32[]{:S(2)}, u32[]{:S(2)}) async-start(f32[64,1,4224]{2,1,0:T(1,128)} %copy.57), calls=%async_computation | async-start | bytes 2162688 | tf_op jit(solution)/shard_map/all_to_all | solution.py:92
  93.0 75.6 %reduce-scatter.2.cloned.1.call-start = ((), (), s32[]{:S(2)}) async-start(), calls=%async_computation.2 | async-start | bytes 73728 | tf_op jit(solution)/shard_map/reduce_scatter | solution.py:137
  93.5 32.3 %copy-start.6 = (f32[16]{0:T(128)}, f32[16]{0:T(128)S(1)}, u32[]{:S(2)}) copy-start(f32[16]{0:T(128)S(1)} %convert_element_type.106) | copy-start | bytes 196
  169.4 17.0 %copy-start.4 = (bf16[16,256]{1,0:T(8,128)(2,1)}, bf16[16,256]{1,0:T(8,128)(2,1)S(1)}, u32[]{:S(2)}) copy-start(bf16[16,256]{1,0:T(8,128)(2,1)S(1)} %get-tuple-element.10) | copy-start | bytes 24580
Sparse Core Ops, SparseCore 0:
  133.5 35.0 reduce-scatter.1
where the time goes:
time: 194 us; the launch traced here: 193 us
  blocking collectives  71.6 us (37%)
  waiting for transfers between devices  59.4 us (31%)
  local copies, waits for them, and re-layouts  25.5 us (13%)
  between operations  14.3 us (7%)
  other arithmetic  11.6 us (6%)
  starting transfers between devices  6.56 us (3%)
  matrix products  4.23 us (2%)
    all_gather x1, blocking collectives, local(): everyone = lax.all_gather(queries, 'req', axis=0, tiled=True)  56 us
    reduce_scatter x1, waiting for transfers between devices, local(): lax.psum_scatter(partial_value.astype(jnp.bfloat16), 'tp', scatter_dimens...  33.2 us
    all_to_all x1, waiting for transfers between devices, local(): arrived = lax.all_to_all(packed, 'req', 0, 0, tiled=True)  26.2 us
    psum x1, blocking collectives, local(): lax.psum((jnp.sum(hidden_mine, -1), jnp.sum(hidden_mine * hidden_mine, -1...  15.6 us
    slice x1, local copies, waits for them, and re-layouts, local(): pool_cache[:, :, 1].reshape(page_count, PAGE, heads_here, HEAD)  10.7 us
    all_to_all x1, starting transfers between devices, local(): arrived = lax.all_to_all(packed, 'req', 0, 0, tiled=True)  6.34 us
    all_to_all x2, local copies, waits for them, and re-layouts, local(): arrived = lax.all_to_all(packed, 'req', 0, 0, tiled=True)  5.25 us
  transfers between devices with their start and end apart: 2, of which 2 were waited for; matrix products, arithmetic and copies ran while one was open for 3% of the time, Pallas kernels for 0%

commit v1 on v0

--- a/solution.py
+++ b/solution.py
@@ -9,6 +9,11 @@
 PAGE = 64
 masked_score = -1e30
 norm_epsilon = 1e-05
+
+
+def tiled_gather(x, axis, dim):
+    copies = jnp.concatenate([x] * lax.axis_size(axis), axis=dim)
+    return lax.all_to_all(copies, axis, dim, dim, tiled=True)
 
 
 def split_halves(values):
@@ -44,7 +49,7 @@
     tail_slots = tail_cache.shape[1]
     n_req = lax.axis_size("req")
     assert group_count == n_req
-    everyone = lax.all_gather(queries, "req", axis=0, tiled=True)
+    everyone = tiled_gather(queries, "req", 0)
     by_group = everyone.reshape(group_count, row_count, heads_here, HEAD)
     safe_group = jnp.clip(page_group, 0, group_count - 1)
     page_queries = by_group[safe_group]

time: 194 us -> 240 us (1.24)
  local copies, waits for them, and re-layouts: 25.5 us -> 109 us
  blocking collectives: 71.6 us -> 15.6 us
  starting transfers between devices: 6.56 us -> 20.1 us
  waiting for transfers between devices: 59.4 us -> 63.9 us
  other arithmetic: 11.6 us -> 8.9 us
    unnamed x16 -> x83, local copies, waits for them, and re-layouts: 0.04 us -> 81.5 us
    all_gather x1 -> x0, blocking collectives: 56 us -> none  [local(): everyone = lax.all_gather(queries, 'req', axis=0, tiled=True)]
    all_to_all x0 -> x1, starting transfers between devices: none -> 13.9 us  [tiled_gather(): return lax.all_to_all(copies, axis, dim, dim, tiled=True)]
    all_to_all x0 -> x1, waiting for transfers between devices: none -> 4.42 us  [tiled_gather(): return lax.all_to_all(copies, axis, dim, dim, tiled=True)]
  transfers between devices with their start and end apart: 2 -> 3, of which waited for: 2 -> 3; matrix products, arithmetic and copies ran while one was open for 3% -> 8% of each run, Pallas kernels for 0% -> 0%
where the time goes in v1:
time: 240 us; the launch traced here: 237 us
  local copies, waits for them, and re-layouts  109 us (45%)
  waiting for transfers between devices  63.9 us (27%)
  starting transfers between devices  20.1 us (8%)
  blocking collectives  15.6 us (6%)
  between operations  14.4 us (6%)
  other arithmetic  8.9 us (4%)
  matrix products  5.45 us (2%)
    unnamed x83, local copies, waits for them, and re-layouts  81.5 us
    reduce_scatter x1, waiting for transfers between devices, local(): lax.psum_scatter(partial_value.astype(jnp.bfloat16), 'tp', scatter_dimens...  33.2 us
    all_to_all x1, waiting for transfers between devices, local(): arrived = lax.all_to_all(packed, 'req', 0, 0, tiled=True)  26.2 us
    psum x1, blocking collectives, local(): lax.psum((jnp.sum(hidden_mine, -1), jnp.sum(hidden_mine * hidden_mine, -1...  15.6 us
    all_to_all x1, starting transfers between devices, tiled_gather(): return lax.all_to_all(copies, axis, dim, dim, tiled=True)  13.9 us
    slice x1, local copies, waits for them, and re-layouts, local(): pool_cache[:, :, 1].reshape(page_count, PAGE, heads_here, HEAD)  12.1 us
    all_to_all x1, starting transfers between devices, local(): arrived = lax.all_to_all(packed, 'req', 0, 0, tiled=True)  6.05 us
    all_to_all x2, local copies, waits for them, and re-layouts, local(): arrived = lax.all_to_all(packed, 'req', 0, 0, tiled=True)  5.25 us
  transfers between devices with their start and end apart: 3, of which 3 were waited for; matrix products, arithmetic and copies ran while one was open for 8% of the time, Pallas kernels for 0%

profile of v1, /device:TPU:2, one launch (start us, length us, event | category | flops | bytes accessed | tf_op | source)
XLA Modules:
  0.0 237.2 jit_solution(11250782179162156290)
XLA Ops:
  7.2 1.4 constant_dynamic-update-slice_fusion.63
  8.6 1.3 constant_dynamic-update-slice_fusion.62
  9.9 1.3 constant_dynamic-update-slice_fusion.61
  12.5 1.3 constant_dynamic-update-slice_fusion.59
  13.7 1.3 constant_dynamic-update-slice_fusion.58
  15.0 1.3 constant_dynamic-update-slice_fusion.57
  16.3 1.3 constant_dynamic-update-slice_fusion.56
  17.6 1.3 constant_dynamic-update-slice_fusion.55
  18.9 1.3 constant_dynamic-update-slice_fusion.54
  20.2 1.3 constant_dynamic-update-slice_fusion.53
  24.1 1.3 constant_dynamic-update-slice_fusion.50
  25.4 1.3 constant_dynamic-update-slice_fusion.49
  26.7 1.3 constant_dynamic-update-slice_fusion.48
  29.3 1.3 constant_dynamic-update-slice_fusion.46
  30.5 1.3 constant_dynamic-update-slice_fusion.45
  31.8 1.3 constant_dynamic-update-slice_fusion.44
  33.1 1.3 constant_dynamic-update-slice_fusion.43
  34.4 1.3 constant_dynamic-update-slice_fusion.42
  35.7 1.3 constant_dynamic-update-slice_fusion.41
  37.0 1.3 constant_dynamic-update-slice_fusion.40
  38.3 1.3 constant_dynamic-update-slice_fusion.39
  39.6 1.3 constant_dynamic-update-slice_fusion.38
  42.2 1.3 constant_dynamic-update-slice_fusion.36
  43.5 1.3 constant_dynamic-update-slice_fusion.35
  44.7 1.3 constant_dynamic-update-slice_fusion.34
  46.0 1.3 constant_dynamic-update-slice_fusion.33
  47.3 1.3 constant_dynamic-update-slice_fusion.32
  48.6 1.3 constant_dynamic-update-slice_fusion.31
  51.2 1.3 constant_dynamic-update-slice_fusion.29
  52.5 1.3 constant_dynamic-update-slice_fusion.28
  55.1 1.3 constant_dynamic-update-slice_fusion.26
  56.4 1.3 constant_dynamic-update-slice_fusion.25
  57.7 1.3 constant_dynamic-update-slice_fusion.24
  60.2 1.3 constant_dynamic-update-slice_fusion.22
  61.5 1.3 constant_dynamic-update-slice_fusion.21
  64.1 1.3 constant_dynamic-update-slice_fusion.19
  65.4 1.3 constant_dynamic-update-slice_fusion.18
  68.0 1.3 constant_dynamic-update-slice_fusion.16
  70.6 1.3 constant_dynamic-update-slice_fusion.14
  71.9 1.3 constant_dynamic-update-slice_fusion.13
  73.1 1.3 constant_dynamic-update-slice_fusion.12
  74.4 1.3 constant_dynamic-update-slice_fusion.11
  75.7 1.3 constant_dynamic-update-slice_fusion.10
  78.3 1.3 constant_dynamic-update-slice_fusion.8
  79.6 1.3 constant_dynamic-update-slice_fusion.7
  80.9 1.3 constant_dynamic-update-slice_fusion.6
  83.5 1.3 constant_dynamic-update-slice_fusion.4
  84.8 1.3 constant_dynamic-update-slice_fusion.3
  86.1 1.3 constant_dynamic-update-slice_fusion.2
  87.4 1.3 constant_dynamic-update-slice_fusion.1
  88.6 1.3 constant_dynamic-update-slice_fusion
  89.9 13.9 %all-to-all-start = ((bf16[64,16,256]{2,1,0:T(8,128)(2,1)}), bf16[64,16,256]{2,1,0:T(8,128)(2,1)S(1)}, u32[]{:S(2)}, u32[]{:S(2)}) async-start(bf16[64,16,256]{2,1,0:T(8,128)(2,1)} %bitcast), calls=%async_computation | async-start | bytes 1048576 | tf_op jit(solution)/shard_map/all_to_all | solution.py:16
  104.9 12.1 %slice_reduce_fusion = (bf16[32,64,256]{2,1,0:T(8,128)(2,1)S(1)}, bf16[32,64,256]{2,1,0:T(8,128)(2,1)}) fusion(bf16[32,64,2,256]{3,2,1,0:T(2,128)(2,1)} %param.17), kind=kLoop, calls=%fused_computation.7 | loop fusion | bytes 4194304 | tf_op jit(solution)/shard_map/slice | solution.py:57
  116.9 4.4 %all-to-all-done = bf16[64,16,256]{2,1,0:T(8,128)(2,1)S(1)} async-done(((bf16[64,16,256]{2,1,0:T(8,128)(2,1)}), bf16[64,16,256]{2,1,0:T(8,128)(2,1)S(1)}, u32[]{:S(2)}, u32[]{:S(2)}) %all-to-all-start) | async-done | bytes 524320 | tf_op jit(solution)/shard_map/all_to_all | solution.py:16
  122.1 2.0 fusion.50
  128.6 2.1 copy.57
  130.8 6.0 %all-to-all-start.1 = ((f32[64,1,4224]{2,1,0:T(1,128)}), f32[64,1,4224]{2,1,0:T(1,128)}, u32[]{:S(2)}, u32[]{:S(2)}) async-start(f32[64,1,4224]{2,1,0:T(1,128)} %copy.57), calls=%async_computation.1 | async-start | bytes 2162688 | tf_op jit(solution)/shard_map/all_to_all | solution.py:97
  137.5 2.2 slice_reduce_fusion.2
  140.0 26.2 %all-to-all-done.1 = f32[64,1,4224]{2,1,0:T(1,128)} async-done(((f32[64,1,4224]{2,1,0:T(1,128)}), f32[64,1,4224]{2,1,0:T(1,128)}, u32[]{:S(2)}, u32[]{:S(2)}) %all-to-all-start.1) | async-done | bytes 1081376 | tf_op jit(solution)/shard_map/all_to_all | solution.py:97
  166.3 3.1 %copy.58 = f32[64,1,4224]{0,2,1:T(8,128)S(1)} copy(f32[64,1,4224]{2,1,0:T(1,128)} %all-to-all-done.1) | data formatting | bytes 2162688 | tf_op jit(solution)/shard_map/all_to_all | solution.py:97
  172.3 1.3 add_add_fusion
  179.3 33.2 %reduce-scatter.2.cloned.1.call-done = bf16[16,256]{1,0:T(8,128)(2,1)} async-done(((bf16[16,2048]{1,0:T(8,128)(2,1)}), bf16[16,256]{1,0:T(8,128)(2,1)}) %reduce-scatter.2.cloned.1.call-update) | async-done | bytes 8208 | tf_op jit(solution)/shard_map/reduce_scatter | solution.py:142
  213.4 15.6 %all-reduce = (f32[16]{0:T(128)S(1)}, f32[16]{0:T(128)S(1)}) all-reduce(f32[16]{0:T(128)S(1)} %get-tuple-element.7, f32[16]{0:T(128)S(1)} %get-tuple-element.6), channel_id=1, replica_groups=mesh['req'=64,'tp'=8] {'tp'}, use_global_device_ids=true, to_apply=%region_12.13 | all-reduce | flops 32 | bytes 256 | tf_op jit(solution)/shard_map/psum | solution.py:149
  229.0 1.4 add_convert_fusion
  (98 shorter events, 33.2 us)
Async XLA Ops:
  7.2 169.2 %copy-start = (bf16[256,2048]{1,0:T(8,128)(2,1)S(1)}, bf16[256,2048]{1,0:T(8,128)(2,1)}, u32[]{:S(2)}) copy-start(bf16[256,2048]{1,0:T(8,128)(2,1)} %param.22) | copy-start | bytes 3145732
  7.2 96.6 %copy-start.6 = (s32[32]{0:T(128)S(1)}, s32[32]{0:T(128)}, u32[]{:S(2)}) copy-start(s32[32]{0:T(128)} %param.18) | copy-start | bytes 388
  7.2 96.7 %copy-start.1 = (s32[64]{0:T(128)S(1)}, s32[64]{0:T(128)}, u32[]{:S(2)}) copy-start(s32[64]{0:T(128)} %param.20) | copy-start | bytes 772
  7.2 97.4 %copy-start.8 = (s32[32]{0:T(128)S(1)}, s32[32]{0:T(128)}, u32[]{:S(2)}) copy-start(s32[32]{0:T(128)} %param.19) | copy-start | bytes 388
  89.9 31.4 %all-to-all-start = ((bf16[64,16,256]{2,1,0:T(8,128)(2,1)}), bf16[64,16,256]{2,1,0:T(8,128)(2,1)S(1)}, u32[]{:S(2)}, u32[]{:S(2)}) async-start(bf16[64,16,256]{2,1,0:T(8,128)(2,1)} %bitcast), calls=%async_computation | async-start | bytes 1048576 | tf_op jit(solution)/shard_map/all_to_all | solution.py:16
  128.6 8.5 %copy-start.2 = (bf16[16,256]{1,0:T(8,128)(2,1)S(1)}, bf16[16,256]{1,0:T(8,128)(2,1)}, u32[]{:S(2)}) copy-start(bf16[16,256]{1,0:T(8,128)(2,1)} %param.13) | copy-start | bytes 24580
  128.6 8.5 %copy-start.4 = (bf16[16,2,256]{2,1,0:T(2,128)(2,1)S(1)}, bf16[16,2,256]{2,1,0:T(2,128)(2,1)}, u32[]{:S(2)}) copy-start(bf16[16,2,256]{2,1,0:T(2,128)(2,1)} %param.14) | copy-start | bytes 49156
  128.6 8.8 %copy-start.9 = (s32[16]{0:T(128)S(1)}, s32[16]{0:T(128)}, u32[]{:S(2)}) copy-start(s32[16]{0:T(128)} %param.16) | copy-start | bytes 196
  128.6 8.9 %copy-start.3 = (bf16[16,32,2,256]{3,2,1,0:T(2,128)(2,1)S(1)}, bf16[16,32,2,256]{3,2,1,0:T(2,128)(2,1)}, u32[]{:S(2)}) copy-start(bf16[16,32,2,256]{3,2,1,0:T(2,128)(2,1)} %param.15) | copy-start | bytes 1572868
  130.8 35.5 %all-to-all-start.1 = ((f32[64,1,4224]{2,1,0:T(1,128)}), f32[64,1,4224]{2,1,0:T(1,128)}, u32[]{:S(2)}, u32[]{:S(2)}) async-start(f32[64,1,4224]{2,1,0:T(1,128)} %copy.57), calls=%async_computation.1 | async-start | bytes 2162688 | tf_op jit(solution)/shard_map/all_to_all | solution.py:97
  136.8 75.7 %reduce-scatter.2.cloned.1.call-start = ((), (), s32[]{:S(2)}) async-start(), calls=%async_computation.3 | async-start | bytes 73728 | tf_op jit(solution)/shard_map/reduce_scatter | solution.py:142
  137.4 32.3 %copy-start.7 = (f32[16]{0:T(128)}, f32[16]{0:T(128)S(1)}, u32[]{:S(2)}) copy-start(f32[16]{0:T(128)S(1)} %convert_element_type.106) | copy-start | bytes 196
  213.4 17.0 %copy-start.5 = (bf16[16,256]{1,0:T(8,128)(2,1)}, bf16[16,256]{1,0:T(8,128)(2,1)S(1)}, u32[]{:S(2)}) copy-start(bf16[16,256]{1,0:T(8,128)(2,1)S(1)} %get-tuple-element.10) | copy-start | bytes 24580
Sparse Core Ops, SparseCore 0:
  177.3 35.1 reduce-scatter.1
